TPU v7x, 512 devices: a whole 4x4x16 slice. The times are simulated.
512 devices in a mesh: dp: 4 (over x), ctx: 16 (over z), mp: 8 (over y, core).
Axes of the slice: x: 4, y: 4, z: 16, core: 2. Of those that a mesh axis runs over, the one named last changes fastest.
Arguments:
- tokens: bfloat16 [4, 2048, 4096], P('dp', 'ctx'), may hold values from -52 to 52
- x_weight: bfloat16 [4096, 8192], P(('dp', 'ctx'), 'mp'), may hold values from -0.09375 to 0.09375
- bc_weight: bfloat16 [4096, 1024], P(('dp', 'ctx'), 'mp'), may hold values from -0.09375 to 0.09375
- dt_weight: bfloat16 [4096, 128], P(('dp', 'ctx'), 'mp'), may hold values from -0.0234375 to 0.0234375
- conv_x: float32 [5, 8192], P(None, 'mp'), may hold values from -0.5 to 0.5
- conv_bc: float32 [5, 1024], P(None, 'mp'), may hold values from -0.5 to 0.5
- dt_bias: float32 [128], P('mp'), may hold values from -4.5 to -2.5
- a_log: float32 [128], P('mp')
- d_skip: float32 [128], P('mp'), may hold values from 0.5 to 1.5
- norm_gain: float32 [8192], P('mp'), may hold values from 0.5 to 1.5
Outputs:
- mixer_out: bfloat16 [4, 2048, 8192], P('dp', 'ctx', 'mp')
- kurtosis: float32 [4096], P('mp')
All inputs are finite; a program needn't handle non-finite values.
Results may differ from a plain program's by a relative error of at most 0.015.
Values may be sent and summed in bfloat16 or wider, within the bound.
No kernel may reach another device: no remote copies, remote signals or barrier semaphores. Data moves between devices by JAX's collectives and lax.ppermute only.
A program may use at most 64 MiB of HBM per device.

v0:
```python
import jax
import jax.numpy as jnp
from jax import lax
from jax.sharding import PartitionSpec as P

ROOT = 64
HEADS = 128
G = 4
NS = 128
HIGH = lax.Precision.HIGHEST
CTX = ("ch", "cl")


def passed_along(value, axis, steps, count):
    first, last = (max(0, -steps), min(count, count - steps))
    return lax.ppermute(value, axis, [(source, source + steps) for source in range(first, last)])


def decay_products(row_decay, targets):
    count = row_decay.shape[0]
    target = lax.broadcasted_iota(jnp.int32, (targets, count, count), 0)
    source = lax.broadcasted_iota(jnp.int32, (targets, count, count), 1)
    between = lax.broadcasted_iota(jnp.int32, (targets, count, count), 2)
    inside = jnp.logical_and(between > source, between < target)
    factors = jnp.where(inside[..., None], row_decay[None, None], 1.0)
    products = jnp.prod(factors, 2)
    return jnp.where((source[:, :, 0] < target[:, :, 0])[..., None], products, 0.0)


def entering(decay, contrib):
    quads, quad = (lax.axis_index("ch"), lax.axis_size("cl"))
    place = lax.axis_index("cl")
    lanes = contrib.shape[-1]
    head_rows = contrib.shape[-2]
    heads = decay.size
    chunk = contrib.size // lanes // quad
    pieces = contrib.reshape(quad, chunk, lanes)
    tail = jnp.zeros((quad, 8, lanes), jnp.float32)
    tail = tail.at[:, 0, :heads].set(jnp.broadcast_to(decay.reshape(1, heads), (quad, heads)))
    outgoing = jnp.concatenate([pieces, tail], 1).astype(jnp.bfloat16)
    incoming = lax.all_to_all(outgoing, "cl", 0, 0).astype(jnp.float32)
    states = incoming[:, :chunk]
    decays = incoming[:, chunk, :heads]
    row_head = (place * chunk + lax.broadcasted_iota(jnp.int32, (chunk, heads), 0)) // head_rows
    pick = row_head == lax.broadcasted_iota(jnp.int32, (chunk, heads), 1)
    row_decay = jnp.sum(jnp.where(pick[None], decays[:, None, :], 0.0), -1)
    local = jnp.einsum("kjr,jrl->krl", decay_products(row_decay, quad + 1), states, precision=HIGH)
    step = lax.broadcasted_iota(jnp.int32, (quad + 1, quad, chunk), 0)
    index = lax.broadcasted_iota(jnp.int32, (quad + 1, quad, chunk), 1)
    entry = jnp.prod(jnp.where(index < step, row_decay[None], 1.0), 1)
    pad_rows = 8 - chunk // lanes % 8
    summary = jnp.concatenate(
        [local[quad], entry[quad].reshape(chunk // lanes, lanes), jnp.zeros((pad_rows, lanes))]
    )
    count_hi = lax.axis_size("ch")
    shared = lax.all_gather(summary.astype(jnp.bfloat16), "ch").astype(jnp.float32)
    totals = shared[:, :chunk]
    quad_decay = shared[:, chunk : chunk + chunk // lanes].reshape(count_hi, chunk)
    earlier = lax.broadcasted_iota(jnp.int32, (count_hi, count_hi, chunk), 0)
    middle = lax.broadcasted_iota(jnp.int32, (count_hi, count_hi, chunk), 1)
    spans = jnp.logical_and(middle > earlier, middle < quads)
    across = jnp.prod(jnp.where(spans, quad_decay[None], 1.0), 1)
    across = jnp.where(earlier[:, 0] < quads, across, 0.0)
    entering_state = jnp.einsum("qr,qrl->rl", across, totals, precision=HIGH)
    carried = local[:quad] + entry[:quad, :, None] * entering_state[None]
    returned = lax.all_to_all(carried.astype(jnp.bfloat16), "cl", 0, 0)
    return returned.astype(jnp.float32).reshape(contrib.shape)


def hadamard_signs(sign_order):
    row_index = lax.broadcasted_iota(jnp.int32, (sign_order, sign_order), 0)
    col_index = lax.broadcasted_iota(jnp.int32, (sign_order, sign_order), 1)
    common = jnp.bitwise_and(row_index, col_index)
    parity = jnp.zeros((sign_order, sign_order), jnp.int32)
    for bit_index in range(sign_order.bit_length() - 1):
        parity = parity + jnp.bitwise_and(jnp.right_shift(common, bit_index), 1)
    return 1.0 - 2.0 * jnp.bitwise_and(parity, 1).astype(jnp.float32)


def kurtosis_from(powers, row_count):
    average = powers[0] / row_count
    second = powers[1] / row_count - average * average
    fourth = (
        powers[3] / row_count
        - 4.0 * average * powers[2] / row_count
        + 6.0 * average * average * powers[1] / row_count
        - 3.0 * average * average * average * average
    )
    return fourth / (second * second + 1e-06)


def shards(
    tokens, x_weight, bc_weight, dt_weight, conv_x, conv_bc, dt_bias, a_log, d_skip, norm_gain
):
    tok_rows = tokens.shape[1]
    model_width = tokens.shape[2]
    signs = hadamard_signs(ROOT)
    blocks = tokens.reshape(tok_rows, ROOT, ROOT)
    first_pass = jnp.einsum(
        "tab,ac->tcb", blocks, signs.astype(jnp.bfloat16), preferred_element_type=jnp.float32
    )
    second = jnp.einsum("tcb,bd->tcd", first_pass, signs, precision=HIGH)
    rotated = (second.reshape(tok_rows, model_width) / ROOT).astype(jnp.bfloat16)
    channel_share = model_width // lax.axis_size("mp")
    own_cols = lax.dynamic_slice_in_dim(
        rotated, lax.axis_index("mp") * channel_share, channel_share, 1
    ).astype(jnp.float32)
    square = own_cols * own_cols
    powers = jnp.stack(
        [
            jnp.sum(own_cols, 0),
            jnp.sum(square, 0),
            jnp.sum(square * own_cols, 0),
            jnp.sum(square * square, 0),
        ]
    )
    ctx_count = lax.axis_size("ch") * lax.axis_size("cl")
    row_count = float(tok_rows * lax.axis_size("dp") * ctx_count)
    totals = lax.psum(lax.psum(powers, CTX), "dp")
    totals, rotated = lax.optimization_barrier((totals, rotated))
    kurtosis = kurtosis_from(totals, row_count)
    local_panel = jnp.concatenate([x_weight, bc_weight, dt_weight], 1)
    panel = lax.all_gather(local_panel, CTX, axis=0, tiled=True)
    seqs = lax.axis_size("dp")
    share = model_width // seqs
    rim = 8
    earlier = passed_along(rotated[tok_rows - rim :], CTX, 1, ctx_count)
    extended = jnp.concatenate([earlier, rotated], 0)
    outgoing = extended.reshape(tok_rows + rim, seqs, share).transpose(1, 0, 2)
    incoming = lax.all_to_all(outgoing, "dp", 0, 0)
    x_end = x_weight.shape[1]
    bc_end = x_end + bc_weight.shape[1]
    side_partials = jnp.einsum(
        "kti,io->kto", incoming, panel[:, x_end:], preferred_element_type=jnp.float32
    )
    side_back = lax.all_to_all(side_partials.astype(jnp.bfloat16), "dp", 0, 0)
    x_partials = jnp.einsum(
        "kti,io->kto", incoming, panel[:, :x_end], preferred_element_type=jnp.float32
    )
    x_back = lax.all_to_all(x_partials.astype(jnp.bfloat16), "dp", 0, 0)
    side_ext = jnp.sum(side_back.astype(jnp.float32), 0)
    x_ext = jnp.sum(x_back.astype(jnp.float32), 0)
    x_cols = x_end
    bc_width = bc_end - x_end
    dt_proj = lax.optimization_barrier(side_ext[rim:, bc_width:].astype(jnp.bfloat16))
    kernel = conv_x.shape[0] - 1

    def causal_conv(rows, taps):
        padded = rows.astype(jnp.bfloat16)[rim - (kernel - 1) :]
        total = taps[kernel]
        for tap_index in range(kernel):
            total = total + taps[tap_index] * padded[tap_index : tap_index + tok_rows]
        return jax.nn.silu(total).astype(jnp.bfloat16)

    bc_own = causal_conv(side_ext[:, :bc_width], conv_bc)
    x_conv = causal_conv(x_ext, conv_x)
    heads_dev = dt_weight.shape[1]
    head_size = x_cols // heads_dev
    per_group = HEADS // G
    groups_here = max(1, heads_dev // per_group)
    heads_local = heads_dev // groups_here
    first_group = lax.axis_index("mp") * heads_dev // per_group
    mp_count = lax.axis_size("mp")
    if bc_own.shape[1] == NS and mp_count == 2 * G and (groups_here == 1):
        owner = [m * heads_dev // per_group for m in range(mp_count)]
        odd_first = [(owner[m] if m % 2 == 0 else G + owner[m], m) for m in range(mp_count)]
        even_first = [(G + owner[m] if m % 2 == 0 else owner[m], m) for m in range(mp_count)]
        got_a = lax.ppermute(bc_own, "mp", odd_first)
        got_b = lax.ppermute(bc_own, "mp", even_first)
        even = lax.axis_index("mp") % 2 == 0
        write_here = jnp.where(even, got_a, got_b).reshape(tok_rows, 1, NS)
        read_here = jnp.where(even, got_b, got_a).reshape(tok_rows, 1, NS)
    else:
        group_all = lax.all_gather(bc_own, "mp", axis=1, tiled=True)
        write_all = group_all[:, : G * NS].reshape(tok_rows, G, NS)
        read_all = group_all[:, G * NS :].reshape(tok_rows, G, NS)
        write_here = lax.dynamic_slice_in_dim(write_all, first_group, groups_here, 1)
        read_here = lax.dynamic_slice_in_dim(read_all, first_group, groups_here, 1)
    step_size = jax.nn.softplus(dt_proj.astype(jnp.float32) + dt_bias)
    decay_rate = step_size * jnp.exp(a_log)
    cumulative = jnp.cumsum(decay_rate, 0)
    block_end = cumulative[-1]
    causal = lax.broadcasted_iota(jnp.int32, (tok_rows, tok_rows), 0) >= lax.broadcasted_iota(
        jnp.int32, (tok_rows, tok_rows), 1
    )
    spread = cumulative.T[:, :, None] - cumulative.T[:, None, :]
    decay_mask = jnp.where(causal, jnp.exp(-jnp.where(causal, spread, 0.0)), 0.0)
    scores = jnp.einsum("tgn,sgn->gts", read_here, write_here, preferred_element_type=jnp.float32)
    weights = (
        scores[:, None]
        * decay_mask.reshape(groups_here, heads_local, tok_rows, tok_rows)
        * step_size.T.reshape(groups_here, heads_local, 1, tok_rows)
    ).astype(jnp.bfloat16)
    x_heads = x_conv.reshape(tok_rows, groups_here, heads_local, head_size)
    within_block = jnp.einsum(
        "ghts,sghp->tghp", weights, x_heads, preferred_element_type=jnp.float32
    )
    update = (
        (jnp.exp(-(block_end - cumulative)) * step_size).reshape(
            tok_rows, groups_here, heads_local
        )[..., None]
        * x_heads
    ).astype(jnp.bfloat16)
    contrib = jnp.einsum("sghp,sgn->ghpn", update, write_here, preferred_element_type=jnp.float32)
    carried = entering(jnp.exp(-block_end).reshape(groups_here, heads_local), contrib)
    from_before = jnp.exp(-cumulative).reshape(tok_rows, groups_here, heads_local)[
        ..., None
    ] * jnp.einsum("tgn,ghpn->tghp", read_here.astype(jnp.float32), carried, precision=HIGH)
    output_raw = (
        within_block
        + from_before
        + d_skip.reshape(groups_here, heads_local)[None, :, :, None] * x_heads.astype(jnp.float32)
    )
    mean_square = jnp.mean(output_raw * output_raw, -1, keepdims=True)
    normed = (
        output_raw
        * lax.rsqrt(mean_square + 1e-05)
        * norm_gain.reshape(groups_here, heads_local, head_size)
    )
    return (normed.reshape(1, tok_rows, x_cols).astype(jnp.bfloat16), kurtosis)


def solution(mesh):
    grid = mesh.devices
    quad = 4 if grid.shape[1] % 4 == 0 else 1
    split = jax.sharding.Mesh(
        grid.reshape(grid.shape[0], grid.shape[1] // quad, quad, grid.shape[2]),
        ("dp", "ch", "cl", "mp"),
    )
    return jax.shard_map(
        shards,
        mesh=split,
        in_specs=(
            P("dp", CTX, None),
            P(("dp",) + CTX, "mp"),
            P(("dp",) + CTX, "mp"),
            P(("dp",) + CTX, "mp"),
            P(None, "mp"),
            P(None, "mp"),
            P("mp"),
            P("mp"),
            P("mp"),
            P("mp"),
        ),
        out_specs=(P("dp", CTX, "mp"), P("mp")),
        check_vma=False,
    )
```

profile of v0, /device:TPU:12, one launch (start us, length us, event | category | flops | bytes accessed | tf_op | source)
XLA Modules:
  0.0 176.9 jit_solution(554264727969521265)
XLA Ops:
  7.2 0.8 copy.129
  8.0 1.6 pad_maximum_fusion.2
  9.6 1.6 copy.123
  11.2 0.9 convolution_bitcast_fusion
  12.1 3.3 %multiply_convert_fusion = bf16[128,64,64]{0,2,1:T(8,128)(2,1)S(1)} fusion(f32[128,64,64]{0,1,2:T(8,128)S(1)} %convolution_bitcast_fusion), kind=kOutput, calls=%fused_computation.4 | convolution fusion | flops 403791872 | bytes 3145728 | tf_op jit(solution)/shard_map/tcb,bd->tcd/dot_general | solution.py:102
  15.5 0.3 convert_reduce_fusion
  15.8 37.2 %psum.14 = f32[4,512]{1,0:T(4,128)S(1)} all-reduce(f32[4,512]{1,0:T(4,128)S(1)} %pad_maximum_fusion.3), channel_id=1, replica_groups=mesh['dp'=4,'ch'=4,'cl'=4,'mp'=8] {'ch','cl'}, use_global_device_ids=true, to_apply=%region_4.0 | all-reduce | flops 2048 | bytes 16384 | tf_op jit(solution)/shard_map/psum | solution.py:119
  53.1 8.5 %psum.15 = f32[4,512]{1,0:T(4,128)S(1)} all-reduce(f32[4,512]{1,0:T(4,128)S(1)} %psum.14), channel_id=1, replica_groups=mesh['dp'=4,'ch'=4,'cl'=4,'mp'=8] {'dp'}, use_global_device_ids=true, to_apply=%region_5.0 | all-reduce | flops 2048 | bytes 16384 | tf_op jit(solution)/shard_map/psum | solution.py:119
  61.5 0.5 copy.126
  62.1 1.7 collective-permute-start
  63.7 2.6 %collective-permute-done = bf16[8,4096]{1,0:T(8,128)(2,1)S(1)} collective-permute-done((bf16[8,4096]{1,0:T(8,128)(2,1)S(1)}, bf16[8,4096]{1,0:T(8,128)(2,1)S(1)}, u32[]{:S(2)}, u32[]{:S(2)}) %collective-permute-start) | collective-permute-done | bytes 65568 | tf_op jit(solution)/shard_map/ppermute | solution.py:16
  66.4 0.1 pad_maximum_fusion
  66.5 1.1 copy.166
  67.6 5.8 %all-to-all-start = ((bf16[4,136,1024]{2,1,0:T(8,128)(2,1)}), bf16[4,136,1024]{2,1,0:T(8,128)(2,1)S(1)}, u32[]{:S(2)}, u32[]{:S(2)}) async-start(bf16[4,136,1024]{2,1,0:T(8,128)(2,1)} %bitcast.108), calls=%async_computation | async-start | bytes 2228224 | tf_op jit(solution)/shard_map/all_to_all | solution.py:130
  73.5 8.2 %all-to-all-done = bf16[4,136,1024]{2,1,0:T(8,128)(2,1)S(1)} async-done(((bf16[4,136,1024]{2,1,0:T(8,128)(2,1)}), bf16[4,136,1024]{2,1,0:T(8,128)(2,1)S(1)}, u32[]{:S(2)}, u32[]{:S(2)}) %all-to-all-start) | async-done | bytes 1114144 | tf_op jit(solution)/shard_map/all_to_all | solution.py:130
  81.7 8.6 %all-gather.2.cloned.1.call-done = bf16[1024,1168]{1,0:T(8,128)(2,1)} async-done(((bf16[64,1168]{1,0:T(8,128)(2,1)}), bf16[1024,1168]{1,0:T(8,128)(2,1)}) %all-gather.2.cloned.1.call-update) | async-done | bytes 2392080 | tf_op jit(solution)/shard_map/all_gather | solution.py:123
  90.3 2.2 %convolution_convert_fusion = bf16[4,136,144]{2,1,0:T(8,128)(2,1)} fusion(bf16[4,136,1024]{2,1,0:T(8,128)(2,1)S(1)} %all-to-all-done, bf16[1024,1168]{1,0:T(8,128)(2,1)} %all-gather.2.cloned.1.call-done), kind=kOutput, calls=%fused_computation.13 | convolution fusion | flops 160510464 | bytes 1795072 | tf_op jit(solution)/shard_map/kti,io->kto/dot_general | solution.py:133
  92.5 4.8 %all-to-all-start.2 = ((bf16[4,136,144]{2,1,0:T(8,128)(2,1)}), bf16[4,136,144]{2,1,0:T(8,128)(2,1)S(1)}, u32[]{:S(2)}, u32[]{:S(2)}) async-start(bf16[4,136,144]{2,1,0:T(8,128)(2,1)} %convolution_convert_fusion), calls=%async_computation.2 | async-start | bytes 557056 | tf_op jit(solution)/shard_map/all_to_all | solution.py:136
  97.3 3.9 %fusion.5 = bf16[4,136,1024]{2,1,0:T(8,128)(2,1)} fusion(bf16[4,136,1024]{2,1,0:T(8,128)(2,1)S(1)} %all-to-all-done, bf16[1024,1168]{1,0:T(8,128)(2,1)} %all-gather.2.cloned.1.call-done), kind=kOutput, calls=%fused_computation.6 | convolution fusion | flops 1141407744 | bytes 4325376 | tf_op jit(solution)/shard_map/kti,io->kto/dot_general | solution.py:137
  101.2 0.7 all-to-all-done.2
  102.0 7.1 %all-to-all-start.1 = ((bf16[4,136,1024]{2,1,0:T(8,128)(2,1)}), bf16[4,136,1024]{2,1,0:T(8,128)(2,1)S(1)}, u32[]{:S(2)}, u32[]{:S(2)}) async-start(bf16[4,136,1024]{2,1,0:T(8,128)(2,1)} %fusion.5), calls=%async_computation.1 | async-start | bytes 2228224 | tf_op jit(solution)/shard_map/all_to_all | solution.py:140
  109.1 0.1 multiply_convert_fusion.6
  109.2 1.9 %collective-permute-start.1 = (bf16[128,128]{1,0:T(8,128)(2,1)S(1)}, bf16[128,128]{1,0:T(8,128)(2,1)S(1)}, u32[]{:S(2)}, u32[]{:S(2)}) collective-permute-start(bf16[128,128]{1,0:T(8,128)(2,1)S(1)} %multiply_convert_fusion.6), channel_id=1, source_target_pairs={{4,0},{0,1},{5,2},{1,3},{6,4},{2,5},{7,6},{3,7},{12,8},{8,9},{13,1... | collective-permute-start | bytes 98312 | tf_op jit(solution)/shard_map/ppermute | solution.py:169
  111.1 3.8 %collective-permute-start.2 = (bf16[128,128]{1,0:T(8,128)(2,1)S(1)}, bf16[128,128]{1,0:T(8,128)(2,1)S(1)}, u32[]{:S(2)}, u32[]{:S(2)}) collective-permute-start(bf16[128,128]{1,0:T(8,128)(2,1)S(1)} %multiply_convert_fusion.6), channel_id=1, source_target_pairs={{0,0},{4,1},{1,2},{5,3},{2,4},{6,5},{3,6},{7,7},{8,8},{12,9},{9,10... | collective-permute-start | bytes 98312 | tf_op jit(solution)/shard_map/ppermute | solution.py:168
  114.9 0.1 copy.151
  115.0 0.1 broadcast_multiply_fusion
  115.1 0.1 copy.133
  115.2 0.2 reduce_window_sum.11
  115.5 0.1 exponential_multiply_fusion
  115.6 1.7 all-to-all-done.1
  117.3 0.2 reduce_sum.79
  117.5 0.4 multiply_convert_fusion.5
  117.9 0.2 copy.130
  118.1 0.1 multiply_convert_fusion.4
  118.2 0.2 convolution_convert_fusion.1
  118.4 0.7 pad_maximum_fusion.1
  119.1 3.4 %all-to-all-start.3 = ((bf16[4,264,128]{2,1,0:T(8,128)(2,1)}), bf16[4,264,128]{2,1,0:T(8,128)(2,1)S(1)}, u32[]{:S(2)}, u32[]{:S(2)}) async-start(bf16[4,264,128]{2,1,0:T(8,128)(2,1)} %pad_maximum_fusion.1), calls=%async_computation.3 | async-start | bytes 540672 | tf_op jit(solution)/shard_map/all_to_all | solution.py:41
  122.6 0.1 copy.138
  122.7 0.1 pad.7.clone
  122.8 8.6 %all-to-all-done.3 = bf16[4,264,128]{2,1,0:T(8,128)(2,1)S(1)} async-done(((bf16[4,264,128]{2,1,0:T(8,128)(2,1)}), bf16[4,264,128]{2,1,0:T(8,128)(2,1)S(1)}, u32[]{:S(2)}, u32[]{:S(2)}) %all-to-all-start.3) | async-done | bytes 270368 | tf_op jit(solution)/shard_map/all_to_all | solution.py:41
  131.5 0.1 select_reduce_fusion.1
  131.6 0.1 select_reduce_fusion
  131.8 0.1 broadcast_select_fusion.6
  131.8 0.3 copy.140
  132.1 1.2 convolution_bitcast_fusion.1
  133.3 0.1 slice.254
  133.5 0.3 maximum_maximum_fusion
  133.9 22.0 %all_gather.8 = bf16[4,264,128]{2,1,0:T(8,128)(2,1)S(1)} all-gather(bf16[1,264,128]{2,1,0:T(8,128)(2,1)S(1)} %copy.142), channel_id=1, replica_groups=mesh['dp'=4,'ch'=4,'cl'=4,'mp'=8] {'ch'}, dimensions={0}, use_global_device_ids=true | all-gather | bytes 337920 | tf_op jit(solution)/shard_map/all_gather | solution.py:56
  155.9 0.1 select_reduce_fusion.3
  156.0 0.1 copy.147
  156.1 0.1 copy.141
  156.3 1.0 fusion.22
  157.3 0.3 fusion.10
  157.7 0.7 copy.143
  158.4 3.5 %all-to-all-start.4 = ((bf16[4,256,128]{2,1,0:T(8,128)(2,1)}), bf16[4,256,128]{2,1,0:T(8,128)(2,1)S(1)}, u32[]{:S(2)}, u32[]{:S(2)}) async-start(bf16[4,256,128]{2,1,0:T(8,128)(2,1)} %copy.143), calls=%async_computation.4 | async-start | bytes 524288 | tf_op jit(solution)/shard_map/all_to_all | solution.py:66
  162.0 0.6 fusion.34
  162.6 0.1 mul.315
  162.8 0.1 fusion.30
  162.9 0.2 copy.144
  163.1 0.5 convolution_bitcast_fusion.3
  163.7 5.0 %all-to-all-done.4 = bf16[4,256,128]{2,1,0:T(8,128)(2,1)S(1)} async-done(((bf16[4,256,128]{2,1,0:T(8,128)(2,1)}), bf16[4,256,128]{2,1,0:T(8,128)(2,1)S(1)}, u32[]{:S(2)}, u32[]{:S(2)}) %all-to-all-start.4) | async-done | bytes 262176 | tf_op jit(solution)/shard_map/all_to_all | solution.py:66
  168.7 0.3 multiply_reduce_fusion
  169.0 0.2 multiply_convert_fusion.3
  169.2 0.9 copy.145
  (51 shorter events, 0.6 us)
Async XLA Ops:
  7.2 83.1 %all-gather.2.cloned.1.call-start = ((), (), s32[]{:S(2)}) async-start(), calls=%async_computation.5 | async-start | bytes 2785280 | tf_op jit(solution)/shard_map/all_gather | solution.py:123
  62.1 4.3 %collective-permute-start = (bf16[8,4096]{1,0:T(8,128)(2,1)S(1)}, bf16[8,4096]{1,0:T(8,128)(2,1)S(1)}, u32[]{:S(2)}, u32[]{:S(2)}) collective-permute-start(bf16[8,4096]{1,0:T(8,128)(2,1)S(1)} %slice.197), channel_id=1, source_target_pairs={{0,8},{8,16},{16,24},{24,32},{32,40},{40,48},{48,56},{56,64},{64,7... | collective-permute-start | bytes 196616 | tf_op jit(solution)/shard_map/ppermute | solution.py:16
  66.5 6.9 %copy-start.5 = (f32[16]{0:T(128)S(1)}, f32[16]{0:T(128)}, u32[]{:S(2)}) copy-start(f32[16]{0:T(128)} %param.19) | copy-start | bytes 196
  66.5 6.9 %copy-start.3 = (f32[5,128]{1,0:T(8,128)S(1)}, f32[5,128]{1,0:T(8,128)}, u32[]{:S(2)}) copy-start(f32[5,128]{1,0:T(8,128)} %param.17) | copy-start | bytes 7684
  66.5 6.9 %copy-start = (f32[5,1024]{1,0:T(8,128)S(1)}, f32[5,1024]{1,0:T(8,128)}, u32[]{:S(2)}) copy-start(f32[5,1024]{1,0:T(8,128)} %param.16) | copy-start | bytes 61444
  67.6 14.1 %all-to-all-start = ((bf16[4,136,1024]{2,1,0:T(8,128)(2,1)}), bf16[4,136,1024]{2,1,0:T(8,128)(2,1)S(1)}, u32[]{:S(2)}, u32[]{:S(2)}) async-start(bf16[4,136,1024]{2,1,0:T(8,128)(2,1)} %bitcast.108), calls=%async_computation | async-start | bytes 2228224 | tf_op jit(solution)/shard_map/all_to_all | solution.py:130
  92.5 9.5 %all-to-all-start.2 = ((bf16[4,136,144]{2,1,0:T(8,128)(2,1)}), bf16[4,136,144]{2,1,0:T(8,128)(2,1)S(1)}, u32[]{:S(2)}, u32[]{:S(2)}) async-start(bf16[4,136,144]{2,1,0:T(8,128)(2,1)} %convolution_convert_fusion), calls=%async_computation.2 | async-start | bytes 557056 | tf_op jit(solution)/shard_map/all_to_all | solution.py:136
  101.2 13.8 %copy-start.2 = (f32[16]{0:T(128)S(1)}, f32[16]{0:T(128)}, u32[]{:S(2)}) copy-start(f32[16]{0:T(128)} %param.18) | copy-start | bytes 196
  102.0 15.3 %all-to-all-start.1 = ((bf16[4,136,1024]{2,1,0:T(8,128)(2,1)}), bf16[4,136,1024]{2,1,0:T(8,128)(2,1)S(1)}, u32[]{:S(2)}, u32[]{:S(2)}) async-start(bf16[4,136,1024]{2,1,0:T(8,128)(2,1)} %fusion.5), calls=%async_computation.1 | async-start | bytes 2228224 | tf_op jit(solution)/shard_map/all_to_all | solution.py:140
  109.2 9.0 %collective-permute-start.1 = (bf16[128,128]{1,0:T(8,128)(2,1)S(1)}, bf16[128,128]{1,0:T(8,128)(2,1)S(1)}, u32[]{:S(2)}, u32[]{:S(2)}) collective-permute-start(bf16[128,128]{1,0:T(8,128)(2,1)S(1)} %multiply_convert_fusion.6), channel_id=1, source_target_pairs={{4,0},{0,1},{5,2},{1,3},{6,4},{2,5},{7,6},{3,7},{12,8},{8,9},{13,1... | collective-permute-start | bytes 98312 | tf_op jit(solution)/shard_map/ppermute | solution.py:169
  111.1 7.1 %collective-permute-start.2 = (bf16[128,128]{1,0:T(8,128)(2,1)S(1)}, bf16[128,128]{1,0:T(8,128)(2,1)S(1)}, u32[]{:S(2)}, u32[]{:S(2)}) collective-permute-start(bf16[128,128]{1,0:T(8,128)(2,1)S(1)} %multiply_convert_fusion.6), channel_id=1, source_target_pairs={{0,0},{4,1},{1,2},{5,3},{2,4},{6,5},{3,6},{7,7},{8,8},{12,9},{9,10... | collective-permute-start | bytes 98312 | tf_op jit(solution)/shard_map/ppermute | solution.py:168
  119.1 12.4 %all-to-all-start.3 = ((bf16[4,264,128]{2,1,0:T(8,128)(2,1)}), bf16[4,264,128]{2,1,0:T(8,128)(2,1)S(1)}, u32[]{:S(2)}, u32[]{:S(2)}) async-start(bf16[4,264,128]{2,1,0:T(8,128)(2,1)} %pad_maximum_fusion.1), calls=%async_computation.3 | async-start | bytes 540672 | tf_op jit(solution)/shard_map/all_to_all | solution.py:41
  133.9 28.7 %copy-start.1 = (f32[1024]{0:T(1024)S(1)}, f32[1024]{0:T(1024)}, u32[]{:S(2)}) copy-start(f32[1024]{0:T(1024)} %param.21) | copy-start | bytes 12292
  158.4 10.3 %copy-start.4 = (f32[16]{0:T(128)S(1)}, f32[16]{0:T(128)}, u32[]{:S(2)}) copy-start(f32[16]{0:T(128)} %param.20) | copy-start | bytes 196
  158.4 10.3 %all-to-all-start.4 = ((bf16[4,256,128]{2,1,0:T(8,128)(2,1)}), bf16[4,256,128]{2,1,0:T(8,128)(2,1)S(1)}, u32[]{:S(2)}, u32[]{:S(2)}) async-start(bf16[4,256,128]{2,1,0:T(8,128)(2,1)} %copy.143), calls=%async_computation.4 | async-start | bytes 524288 | tf_op jit(solution)/shard_map/all_to_all | solution.py:66
Sparse Core Ops, SparseCore 0:
  10.7 79.5 all-gather.1
where the time goes:
time: 178 us; the launch traced here: 177 us
  blocking collectives  67.7 us (38%)
  waiting for transfers between devices  35.6 us (20%)
  starting transfers between devices  32.1 us (18%)
  between operations  14.5 us (8%)
  matrix products  13.8 us (8%)
  local copies, waits for them, and re-layouts  7.35 us (4%)
  other arithmetic  5.94 us (3%)
    psum x2, blocking collectives, shards(): totals = lax.psum(lax.psum(powers, CTX), 'dp')  45.7 us
    all_gather x1, blocking collectives, entering(): lax.all_gather(summary.astype(jnp.bfloat16), 'ch').astype(jnp.float32)  22 us
    all_to_all x1, waiting for transfers between devices, entering(): incoming = lax.all_to_all(outgoing, 'cl', 0, 0).astype(jnp.float32)  8.64 us
    all_gather x1, waiting for transfers between devices, shards(): panel = lax.all_gather(local_panel, CTX, axis=0, tiled=True)  8.63 us
    all_to_all x1, waiting for transfers between devices, shards(): incoming = lax.all_to_all(outgoing, 'dp', 0, 0)  8.2 us
    all_to_all x1, starting transfers between devices, shards(): x_back = lax.all_to_all(x_partials.astype(jnp.bfloat16), 'dp', 0, 0)  7.06 us
    all_to_all x1, starting transfers between devices, shards(): incoming = lax.all_to_all(outgoing, 'dp', 0, 0)  5.79 us
    all_to_all x1, waiting for transfers between devices, entering(): returned = lax.all_to_all(carried.astype(jnp.bfloat16), 'cl', 0, 0)  5.05 us
  transfers between devices with their start and end apart: 9, of which 7 were waited for; matrix products, arithmetic and copies ran while one was open for 9% of the time, Pallas kernels for 0%

commit v1 on v0

--- a/solution.py
+++ b/solution.py
@@ -9,6 +9,13 @@
 NS = 128
 HIGH = lax.Precision.HIGHEST
 CTX = ("ch", "cl")
+
+
+def exchange_gather(array, axis, d):
+    n_dev = lax.axis_size(axis)
+    blocks = jnp.stack([array for _ in range(n_dev)])
+    blocks = lax.all_to_all(blocks, axis, split_axis=0, concat_axis=0)
+    return jnp.concatenate(blocks, axis=d)
 
 
 def passed_along(value, axis, steps, count):
@@ -120,7 +127,7 @@
     totals, rotated = lax.optimization_barrier((totals, rotated))
     kurtosis = kurtosis_from(totals, row_count)
     local_panel = jnp.concatenate([x_weight, bc_weight, dt_weight], 1)
-    panel = lax.all_gather(local_panel, CTX, axis=0, tiled=True)
+    panel = exchange_gather(local_panel, CTX, 0)
     seqs = lax.axis_size("dp")
     share = model_width // seqs
     rim = 8

time: 178 us -> 273 us (1.53)
  the two profiles are of different devices: /device:TPU:12 before, /device:TPU:16 now
where the time goes in v1:
time: 273 us; the launch traced here: 272 us
  waiting for transfers between devices  138 us (51%)
  blocking collectives  71.1 us (26%)
  starting transfers between devices  35.6 us (13%)
  matrix products  13.6 us (5%)
  local copies, waits for them, and re-layouts  8.5 us (3%)
  other arithmetic  4.33 us (2%)
    all_to_all x1, waiting for transfers between devices, exchange_gather(): blocks = lax.all_to_all(blocks, axis, split_axis=0, concat_axis=0)  103 us
    psum x2, blocking collectives, shards(): totals = lax.psum(lax.psum(powers, CTX), 'dp')  47.6 us
    all_gather x1, blocking collectives, entering(): lax.all_gather(summary.astype(jnp.bfloat16), 'ch').astype(jnp.float32)  23.4 us
    all_to_all x1, waiting for transfers between devices, shards(): incoming = lax.all_to_all(outgoing, 'dp', 0, 0)  11.1 us
    all_to_all x1, starting transfers between devices, exchange_gather(): blocks = lax.all_to_all(blocks, axis, split_axis=0, concat_axis=0)  10.6 us
    all_to_all x1, waiting for transfers between devices, shards(): x_back = lax.all_to_all(x_partials.astype(jnp.bfloat16), 'dp', 0, 0)  6.94 us
    all_to_all x1, waiting for transfers between devices, entering(): incoming = lax.all_to_all(outgoing, 'cl', 0, 0).astype(jnp.float32)  6.57 us
  transfers between devices with their start and end apart: 9, of which 7 were waited for; matrix products, arithmetic and copies ran while one was open for 3% of the time, Pallas kernels for 0%

profile of v1, /device:TPU:16, one launch (start us, length us, event | category | flops | bytes accessed | tf_op | source)
XLA Modules:
  0.0 272.3 jit_solution(4776929350491539314)
XLA Ops:
  0.6 1.6 copy.123
  2.3 0.9 convolution_bitcast_fusion
  3.2 3.3 %multiply_convert_fusion = bf16[128,64,64]{0,2,1:T(8,128)(2,1)S(1)} fusion(f32[128,64,64]{0,1,2:T(8,128)S(1)} %convolution_bitcast_fusion), kind=kOutput, calls=%fused_computation.4 | convolution fusion | flops 403791872 | bytes 3145728 | tf_op jit(solution)/shard_map/tcb,bd->tcd/dot_general | solution.py:109
  6.5 0.3 convert_reduce_fusion
  6.8 37.0 %psum.14 = f32[4,512]{1,0:T(4,128)S(1)} all-reduce(f32[4,512]{1,0:T(4,128)S(1)} %pad_maximum_fusion.3), channel_id=1, replica_groups=mesh['dp'=4,'ch'=4,'cl'=4,'mp'=8] {'ch','cl'}, use_global_device_ids=true, to_apply=%region_4.0 | all-reduce | flops 2048 | bytes 16384 | tf_op jit(solution)/shard_map/psum | solution.py:126
  43.9 10.6 %psum.15 = f32[4,512]{1,0:T(4,128)S(1)} all-reduce(f32[4,512]{1,0:T(4,128)S(1)} %psum.14), channel_id=1, replica_groups=mesh['dp'=4,'ch'=4,'cl'=4,'mp'=8] {'dp'}, use_global_device_ids=true, to_apply=%region_5.0 | all-reduce | flops 2048 | bytes 16384 | tf_op jit(solution)/shard_map/psum | solution.py:126
  54.5 0.5 copy.126
  55.0 1.7 collective-permute-start
  56.7 1.9 collective-permute-done
  58.6 0.1 pad_maximum_fusion
  58.7 1.1 copy.166
  59.8 3.5 %all-to-all-start = ((bf16[4,136,1024]{2,1,0:T(8,128)(2,1)}), bf16[4,136,1024]{2,1,0:T(8,128)(2,1)S(1)}, u32[]{:S(2)}, u32[]{:S(2)}) async-start(bf16[4,136,1024]{2,1,0:T(8,128)(2,1)} %bitcast.109), calls=%async_computation | async-start | bytes 2228224 | tf_op jit(solution)/shard_map/all_to_all | solution.py:137
  63.3 0.1 copy.129
  63.5 11.1 %all-to-all-done = bf16[4,136,1024]{2,1,0:T(8,128)(2,1)S(1)} async-done(((bf16[4,136,1024]{2,1,0:T(8,128)(2,1)}), bf16[4,136,1024]{2,1,0:T(8,128)(2,1)S(1)}, u32[]{:S(2)}, u32[]{:S(2)}) %all-to-all-start) | async-done | bytes 1114144 | tf_op jit(solution)/shard_map/all_to_all | solution.py:137
  74.5 1.8 stack.17
  76.4 10.6 %all-to-all-start.1 = ((bf16[16,64,1168]{2,1,0:T(8,128)(2,1)}), bf16[16,64,1168]{2,1,0:T(8,128)(2,1)S(1)}, u32[]{:S(2)}, u32[]{:S(2)}) async-start(bf16[16,64,1168]{2,1,0:T(8,128)(2,1)} %stack.17), calls=%async_computation.1 | async-start | bytes 5242880 | tf_op jit(solution)/shard_map/all_to_all | solution.py:17
  87.2 103.3 %all-to-all-done.1 = bf16[16,64,1168]{2,1,0:T(8,128)(2,1)S(1)} async-done(((bf16[16,64,1168]{2,1,0:T(8,128)(2,1)}), bf16[16,64,1168]{2,1,0:T(8,128)(2,1)S(1)}, u32[]{:S(2)}, u32[]{:S(2)}) %all-to-all-start.1) | async-done | bytes 2392096 | tf_op jit(solution)/shard_map/all_to_all | solution.py:17
  190.5 2.4 convolution_convert_fusion
  192.9 3.4 %all-to-all-start.3 = ((bf16[4,136,144]{2,1,0:T(8,128)(2,1)}), bf16[4,136,144]{2,1,0:T(8,128)(2,1)S(1)}, u32[]{:S(2)}, u32[]{:S(2)}) async-start(bf16[4,136,144]{2,1,0:T(8,128)(2,1)} %convolution_convert_fusion), calls=%async_computation.3 | async-start | bytes 557056 | tf_op jit(solution)/shard_map/all_to_all | solution.py:143
  196.3 3.6 %fusion.5 = bf16[4,136,1024]{2,1,0:T(8,128)(2,1)} fusion(bf16[4,136,1024]{2,1,0:T(8,128)(2,1)} %copy-done, bf16[1024,1168]{1,0:T(8,128)(2,1)S(1)} %bitcast.116), kind=kOutput, calls=%fused_computation.6 | convolution fusion | flops 1141407744 | bytes 4325376 | tf_op jit(solution)/shard_map/kti,io->kto/dot_general | solution.py:144
  199.9 3.2 %all-to-all-done.3 = bf16[4,136,144]{2,1,0:T(8,128)(2,1)S(1)} async-done(((bf16[4,136,144]{2,1,0:T(8,128)(2,1)}), bf16[4,136,144]{2,1,0:T(8,128)(2,1)S(1)}, u32[]{:S(2)}, u32[]{:S(2)}) %all-to-all-start.3) | async-done | bytes 156704 | tf_op jit(solution)/shard_map/all_to_all | solution.py:143
  203.1 3.5 %all-to-all-start.2 = ((bf16[4,136,1024]{2,1,0:T(8,128)(2,1)}), bf16[4,136,1024]{2,1,0:T(8,128)(2,1)S(1)}, u32[]{:S(2)}, u32[]{:S(2)}) async-start(bf16[4,136,1024]{2,1,0:T(8,128)(2,1)} %fusion.5), calls=%async_computation.2 | async-start | bytes 2228224 | tf_op jit(solution)/shard_map/all_to_all | solution.py:147
  206.7 0.1 multiply_convert_fusion.6
  206.7 2.2 collective-permute-start.1
  209.0 1.9 collective-permute-start.2
  211.0 0.1 broadcast_multiply_fusion
  211.1 0.1 copy.133
  211.2 0.2 reduce_window_sum.11
  211.5 0.1 exponential_multiply_fusion
  211.6 6.9 %all-to-all-done.2 = bf16[4,136,1024]{2,1,0:T(8,128)(2,1)S(1)} async-done(((bf16[4,136,1024]{2,1,0:T(8,128)(2,1)}), bf16[4,136,1024]{2,1,0:T(8,128)(2,1)S(1)}, u32[]{:S(2)}, u32[]{:S(2)}) %all-to-all-start.2) | async-done | bytes 1114144 | tf_op jit(solution)/shard_map/all_to_all | solution.py:147
  218.5 0.2 reduce_sum.79
  218.7 0.4 multiply_convert_fusion.5
  219.1 0.2 copy.130
  219.3 0.1 multiply_convert_fusion.4
  219.4 0.2 convolution_convert_fusion.1
  219.6 0.7 pad_maximum_fusion.1
  220.3 5.1 %all-to-all-start.4 = ((bf16[4,264,128]{2,1,0:T(8,128)(2,1)}), bf16[4,264,128]{2,1,0:T(8,128)(2,1)S(1)}, u32[]{:S(2)}, u32[]{:S(2)}) async-start(bf16[4,264,128]{2,1,0:T(8,128)(2,1)} %pad_maximum_fusion.1), calls=%async_computation.4 | async-start | bytes 540672 | tf_op jit(solution)/shard_map/all_to_all | solution.py:48
  225.4 0.1 copy.138
  225.5 0.1 pad.7.clone
  225.7 6.6 %all-to-all-done.4 = bf16[4,264,128]{2,1,0:T(8,128)(2,1)S(1)} async-done(((bf16[4,264,128]{2,1,0:T(8,128)(2,1)}), bf16[4,264,128]{2,1,0:T(8,128)(2,1)S(1)}, u32[]{:S(2)}, u32[]{:S(2)}) %all-to-all-start.4) | async-done | bytes 270368 | tf_op jit(solution)/shard_map/all_to_all | solution.py:48
  232.3 0.1 select_reduce_fusion.1
  232.4 0.1 select_reduce_fusion
  232.5 0.1 broadcast_select_fusion.6
  232.6 0.3 copy.140
  232.9 1.2 convolution_bitcast_fusion.1
  234.1 0.1 slice.254
  234.3 0.3 maximum_maximum_fusion
  234.6 23.4 %all_gather.4 = bf16[4,264,128]{2,1,0:T(8,128)(2,1)S(1)} all-gather(bf16[1,264,128]{2,1,0:T(8,128)(2,1)S(1)} %copy.142), channel_id=1, replica_groups=mesh['dp'=4,'ch'=4,'cl'=4,'mp'=8] {'ch'}, dimensions={0}, use_global_device_ids=true | all-gather | bytes 337920 | tf_op jit(solution)/shard_map/all_gather | solution.py:63
  258.1 0.1 select_reduce_fusion.3
  258.2 0.1 copy.147
  258.4 0.1 copy.141
  258.5 1.0 fusion.22
  259.6 0.3 fusion.10
  259.9 0.7 copy.143
  260.7 3.5 %all-to-all-start.5 = ((bf16[4,256,128]{2,1,0:T(8,128)(2,1)}), bf16[4,256,128]{2,1,0:T(8,128)(2,1)S(1)}, u32[]{:S(2)}, u32[]{:S(2)}) async-start(bf16[4,256,128]{2,1,0:T(8,128)(2,1)} %copy.143), calls=%async_computation.5 | async-start | bytes 524288 | tf_op jit(solution)/shard_map/all_to_all | solution.py:73
  264.2 0.6 fusion.34
  264.8 0.1 mul.315
  265.0 0.1 fusion.30
  265.2 0.2 copy.144
  265.4 0.5 convolution_bitcast_fusion.3
  265.9 5.0 %all-to-all-done.5 = bf16[4,256,128]{2,1,0:T(8,128)(2,1)S(1)} async-done(((bf16[4,256,128]{2,1,0:T(8,128)(2,1)}), bf16[4,256,128]{2,1,0:T(8,128)(2,1)S(1)}, u32[]{:S(2)}, u32[]{:S(2)}) %all-to-all-start.5) | async-done | bytes 262176 | tf_op jit(solution)/shard_map/all_to_all | solution.py:73
  270.9 0.3 multiply_reduce_fusion
  271.3 0.2 multiply_convert_fusion.3
  271.5 0.9 copy.145
  (59 shorter events, 0.6 us)
Async XLA Ops:
  55.0 3.6 %collective-permute-start = (bf16[8,4096]{1,0:T(8,128)(2,1)S(1)}, bf16[8,4096]{1,0:T(8,128)(2,1)S(1)}, u32[]{:S(2)}, u32[]{:S(2)}) collective-permute-start(bf16[8,4096]{1,0:T(8,128)(2,1)S(1)} %slice.197), channel_id=1, source_target_pairs={{0,8},{8,16},{16,24},{24,32},{32,40},{40,48},{48,56},{56,64},{64,7... | collective-permute-start | bytes 196616 | tf_op jit(solution)/shard_map/ppermute | solution.py:23
  58.7 4.6 %copy-start.4 = (bf16[64,16]{0,1:T(8,128)(2,1)S(1)}, bf16[64,16]{0,1:T(8,128)(2,1)}, u32[]{:S(2)}) copy-start(bf16[64,16]{0,1:T(8,128)(2,1)} %param.15) | copy-start | bytes 6148
  58.7 4.7 %copy-start.1 = (bf16[64,1024]{1,0:T(8,128)(2,1)S(1)}, bf16[64,1024]{1,0:T(8,128)(2,1)}, u32[]{:S(2)}) copy-start(bf16[64,1024]{1,0:T(8,128)(2,1)} %param.13) | copy-start | bytes 393220
  58.7 4.7 %copy-start.2 = (bf16[64,128]{1,0:T(8,128)(2,1)S(1)}, bf16[64,128]{1,0:T(8,128)(2,1)}, u32[]{:S(2)}) copy-start(bf16[64,128]{1,0:T(8,128)(2,1)} %param.14) | copy-start | bytes 49156
  59.8 14.7 %all-to-all-start = ((bf16[4,136,1024]{2,1,0:T(8,128)(2,1)}), bf16[4,136,1024]{2,1,0:T(8,128)(2,1)S(1)}, u32[]{:S(2)}, u32[]{:S(2)}) async-start(bf16[4,136,1024]{2,1,0:T(8,128)(2,1)} %bitcast.109), calls=%async_computation | async-start | bytes 2228224 | tf_op jit(solution)/shard_map/all_to_all | solution.py:137
  74.5 1.8 copy-start
  76.4 10.7 %copy-start.9 = (f32[16]{0:T(128)S(1)}, f32[16]{0:T(128)}, u32[]{:S(2)}) copy-start(f32[16]{0:T(128)} %param.19) | copy-start | bytes 196
  76.4 10.7 %copy-start.7 = (f32[5,128]{1,0:T(8,128)S(1)}, f32[5,128]{1,0:T(8,128)}, u32[]{:S(2)}) copy-start(f32[5,128]{1,0:T(8,128)} %param.17) | copy-start | bytes 7684
  76.4 10.7 %copy-start.3 = (f32[5,1024]{1,0:T(8,128)S(1)}, f32[5,1024]{1,0:T(8,128)}, u32[]{:S(2)}) copy-start(f32[5,1024]{1,0:T(8,128)} %param.16) | copy-start | bytes 61444
  76.4 114.1 %all-to-all-start.1 = ((bf16[16,64,1168]{2,1,0:T(8,128)(2,1)}), bf16[16,64,1168]{2,1,0:T(8,128)(2,1)S(1)}, u32[]{:S(2)}, u32[]{:S(2)}) async-start(bf16[16,64,1168]{2,1,0:T(8,128)(2,1)} %stack.17), calls=%async_computation.1 | async-start | bytes 5242880 | tf_op jit(solution)/shard_map/all_to_all | solution.py:17
  192.9 10.2 %all-to-all-start.3 = ((bf16[4,136,144]{2,1,0:T(8,128)(2,1)}), bf16[4,136,144]{2,1,0:T(8,128)(2,1)S(1)}, u32[]{:S(2)}, u32[]{:S(2)}) async-start(bf16[4,136,144]{2,1,0:T(8,128)(2,1)} %convolution_convert_fusion), calls=%async_computation.3 | async-start | bytes 557056 | tf_op jit(solution)/shard_map/all_to_all | solution.py:143
  199.9 11.1 %copy-start.6 = (f32[16]{0:T(128)S(1)}, f32[16]{0:T(128)}, u32[]{:S(2)}) copy-start(f32[16]{0:T(128)} %param.18) | copy-start | bytes 196
  203.1 15.4 %all-to-all-start.2 = ((bf16[4,136,1024]{2,1,0:T(8,128)(2,1)}), bf16[4,136,1024]{2,1,0:T(8,128)(2,1)S(1)}, u32[]{:S(2)}, u32[]{:S(2)}) async-start(bf16[4,136,1024]{2,1,0:T(8,128)(2,1)} %fusion.5), calls=%async_computation.2 | async-start | bytes 2228224 | tf_op jit(solution)/shard_map/all_to_all | solution.py:147
  206.7 12.6 %collective-permute-start.1 = (bf16[128,128]{1,0:T(8,128)(2,1)S(1)}, bf16[128,128]{1,0:T(8,128)(2,1)S(1)}, u32[]{:S(2)}, u32[]{:S(2)}) collective-permute-start(bf16[128,128]{1,0:T(8,128)(2,1)S(1)} %multiply_convert_fusion.6), channel_id=1, source_target_pairs={{4,0},{0,1},{5,2},{1,3},{6,4},{2,5},{7,6},{3,7},{12,8},{8,9},{13,1... | collective-permute-start | bytes 98312 | tf_op jit(solution)/shard_map/ppermute | solution.py:176
  209.0 10.4 %collective-permute-start.2 = (bf16[128,128]{1,0:T(8,128)(2,1)S(1)}, bf16[128,128]{1,0:T(8,128)(2,1)S(1)}, u32[]{:S(2)}, u32[]{:S(2)}) collective-permute-start(bf16[128,128]{1,0:T(8,128)(2,1)S(1)} %multiply_convert_fusion.6), channel_id=1, source_target_pairs={{0,0},{4,1},{1,2},{5,3},{2,4},{6,5},{3,6},{7,7},{8,8},{12,9},{9,10... | collective-permute-start | bytes 98312 | tf_op jit(solution)/shard_map/ppermute | solution.py:175
  220.3 11.9 %all-to-all-start.4 = ((bf16[4,264,128]{2,1,0:T(8,128)(2,1)}), bf16[4,264,128]{2,1,0:T(8,128)(2,1)S(1)}, u32[]{:S(2)}, u32[]{:S(2)}) async-start(bf16[4,264,128]{2,1,0:T(8,128)(2,1)} %pad_maximum_fusion.1), calls=%async_computation.4 | async-start | bytes 540672 | tf_op jit(solution)/shard_map/all_to_all | solution.py:48
  234.6 30.2 %copy-start.5 = (f32[1024]{0:T(1024)S(1)}, f32[1024]{0:T(1024)}, u32[]{:S(2)}) copy-start(f32[1024]{0:T(1024)} %param.21) | copy-start | bytes 12292
  260.7 10.3 %copy-start.8 = (f32[16]{0:T(128)S(1)}, f32[16]{0:T(128)}, u32[]{:S(2)}) copy-start(f32[16]{0:T(128)} %param.20) | copy-start | bytes 196
  260.7 10.3 %all-to-all-start.5 = ((bf16[4,256,128]{2,1,0:T(8,128)(2,1)}), bf16[4,256,128]{2,1,0:T(8,128)(2,1)S(1)}, u32[]{:S(2)}, u32[]{:S(2)}) async-start(bf16[4,256,128]{2,1,0:T(8,128)(2,1)} %copy.143), calls=%async_computation.5 | async-start | bytes 524288 | tf_op jit(solution)/shard_map/all_to_all | solution.py:73
